TPU v7x, 512 devices: a whole 4x4x16 slice. The times are simulated.
512 devices in a mesh: front: 4 (over y), row: 4 (over x), col: 32 (over z, core).
Axes of the slice: x: 4, y: 4, z: 16, core: 2. Of those that a mesh axis runs over, the one named last changes fastest.
Arguments:
- inverse_factor: bfloat16 [4, 1024, 1024], P('front', ('row', 'col')), as said below
- panel: bfloat16 [4, 8192, 1024], P('front', 'row', 'col'), may hold values from -1.1953125 to 1.1953125
- trailing: float32 [4, 8192, 8192], P('front', 'row', 'col'), may hold values from -6 to 6
- extend_map: int32 [4, 512], P('front'), may hold values from 0 to 511, as said below
Outputs:
- parent_update: float32 [4, 4096, 8192], P('front', 'row', 'col')
Inputs may be any that keep to these rules, and one draw needn't show every extreme that they name: Each inverse_factor[f] is upper triangular with positive diagonal. Each row of extend_map is a permutation of 0 to 511, and extend_map[f, q] % (128) == q % 128.
All inputs are finite; a program needn't handle non-finite values.
Results may differ from a plain program's by a relative error of at most 0.0034.
Values may be sent and summed in bfloat16 or wider, within the bound.
No kernel may reach another device: no remote copies, remote signals or barrier semaphores. Data moves between devices by JAX's collectives and lax.ppermute only.
A program may use at most 64 MiB of HBM per device.

v0:
```python
import jax
import jax.numpy as jnp
from jax import lax
from jax.sharding import Mesh
from jax.sharding import PartitionSpec as P


def from_partner(value, axis, distance):
    mask = 2**distance
    pairs = [(source, source ^ mask) for source in range(lax.axis_size(axis))]
    return lax.ppermute(value, axis, pairs)


def outer_rows(left, right):
    return lax.dot_general(
        left, right, (((1,), (1,)), ((), ())), preferred_element_type=jnp.float32
    )


def ring_gather(value, axis, index, n):
    ahead = [(source, (source + 1) % n) for source in range(n)]
    behind = [(source, (source - 1) % n) for source in range(n)]
    held = [value]
    forward = value
    backward = value
    for step in range(1, n):
        if step % 2:
            forward = lax.ppermute(forward, axis, ahead)
            held.append(forward)
        else:
            backward = lax.ppermute(backward, axis, behind)
            held.append(backward)
    offsets = [0] + [(step + 1) // 2 if step % 2 else -(step // 2) for step in range(1, n)]
    by_offset = [None] * n
    for offset, block in zip(offsets, held):
        by_offset[offset % n] = block
    stacked = jnp.stack(by_offset)
    sources = jnp.arange(n, dtype=jnp.int32)
    return stacked[(index - sources) % n]


def inverse_order(target):
    slots = jnp.arange(target.shape[0], dtype=jnp.int32)
    hit = target[None, :] == slots[:, None]
    return jnp.sum(jnp.where(hit, slots[None, :], 0), axis=1, dtype=jnp.int32)


def local(inverse_factor, panel, trailing, extend_map):
    nrow = lax.axis_size("row")
    nz = lax.axis_size("z")
    ncore = lax.axis_size("core")
    ncol = nz * ncore
    group = nrow * ncol
    row_index = lax.axis_index("row")
    col_index = lax.axis_index("z") * ncore + lax.axis_index("core")
    inverse = lax.all_gather(inverse_factor[0], "core", axis=0, tiled=True)
    inverse = lax.all_gather(inverse, "z", axis=0, tiled=True)
    inverse = ring_gather(inverse, "row", row_index, nrow)
    order = inverse.shape[-1]
    inverse = inverse.reshape(order, order)
    columns = lax.all_gather(panel[0], ("z", "core"), axis=1, tiled=True)

    def solve(rows):
        return jnp.dot(rows, inverse, preferred_element_type=jnp.float32).astype(jnp.bfloat16)

    local_trailing = trailing[0]
    rows_here = local_trailing.shape[0]
    cols_here = local_trailing.shape[1]
    share = rows_here // ncol
    piece = solve(lax.dynamic_slice_in_dim(columns, col_index * share, share, 0))
    block_map = extend_map[0]
    nblocks = block_map.shape[0]
    per_class = nblocks // group
    width = rows_here // (ncol * per_class)
    slots_row = jnp.arange(ncol * per_class, dtype=jnp.int32)
    class_row = slots_row // per_class
    depth_row = slots_row % per_class
    source_row = (depth_row * ncol + class_row) * nrow + row_index
    target_row = class_row * per_class + block_map[source_row] // group
    gather_row = inverse_order(target_row)
    slots_col = jnp.arange(nrow * per_class, dtype=jnp.int32)
    class_col = slots_col // per_class
    depth_col = slots_col % per_class
    source_col = (depth_col * ncol + col_index) * nrow + class_col
    target_col = class_col * per_class + block_map[source_col] // group
    gather_col = inverse_order(target_col)
    own_blocks = (
        lax.dynamic_slice_in_dim(gather_col, row_index * per_class, per_class, 0)
        - row_index * per_class
    )
    copies = jnp.tile(own_blocks, nrow)
    piece = piece.reshape(per_class, width, order)[copies].reshape(nrow, share, order)
    col_side = lax.all_to_all(piece, "row", 0, 0, tiled=True).reshape(cols_here, order)
    blocks_col = slots_col[:, None] == gather_col[None, :]
    same = jnp.arange(width)[:, None] == jnp.arange(width)[None, :]
    select_cols = (
        (blocks_col[:, None, :, None] & same[None, :, None, :])
        .reshape(cols_here, cols_here)
        .astype(jnp.float32)
    )
    solved = solve(columns)
    member = lax.axis_index("front") % 2
    half = rows_here // 2
    half_blocks = half // width

    def half_update(which):
        rows = lax.dynamic_slice_in_dim(local_trailing, which * half, half, 0)
        low = lax.dynamic_slice_in_dim(solved, which * half, half, 0)
        rows, low = lax.optimization_barrier((rows, low))
        moved_cols = jnp.dot(
            rows, select_cols, precision=lax.Precision.HIGHEST, preferred_element_type=jnp.float32
        )
        schur = moved_cols - outer_rows(low, col_side)
        blocks = (
            lax.dynamic_slice_in_dim(gather_row, which * half_blocks, half_blocks, 0)
            - which * half_blocks
        )
        return schur.reshape(half_blocks, width, cols_here)[blocks].reshape(half, cols_here)

    outgoing = half_update(1 - member).astype(jnp.bfloat16)
    incoming = from_partner(outgoing, "front", 0)
    keep = half_update(member)
    return (keep + incoming.astype(jnp.float32))[None]


def solution(mesh):
    devices = mesh.devices
    shape = devices.shape
    fine = Mesh(
        devices.reshape(shape[0], shape[1], shape[2] // 2, 2), ("front", "row", "z", "core")
    )
    cols = ("z", "core")
    return jax.shard_map(
        local,
        mesh=fine,
        in_specs=(
            P("front", ("row",) + cols, None),
            P("front", "row", cols),
            P("front", "row", cols),
            P("front", None),
        ),
        out_specs=P("front", "row", cols),
        check_vma=False,
    )
```

profile of v0, /device:TPU:2, one launch (start us, length us, event | category | flops | bytes accessed | tf_op | source)
XLA Modules:
  0.0 133.4 jit_solution(17239717450245742176)
XLA Ops:
  6.5 0.0 copy-start
  6.5 0.0 copy-start.3
  6.5 0.0 all-gather.5.cloned.1.call-start
  6.5 0.7 all-gather.5.cloned.1.call-update
  7.3 2.0 %all-gather = bf16[1,16,1024]{2,1,0:T(8,128)(2,1)S(1)} all-gather(bf16[1,8,1024]{2,1,0:T(8,128)(2,1)} %param.4), channel_id=2, replica_groups=mesh['front'=4,'row'=4,'z'=16,'core'=2] {'core'}, dimensions={1}, use_global_device_ids=true | all-gather | bytes 49152 | tf_op jit(solution)/shard_map/all_gather | solution.py:56
  9.3 38.4 %all-gather.1 = bf16[1,256,1024]{2,1,0:T(8,128)(2,1)S(1)} all-gather(bf16[1,16,1024]{2,1,0:T(8,128)(2,1)S(1)} %all-gather), channel_id=3, replica_groups=mesh['front'=4,'row'=4,'z'=16,'core'=2] {'z'}, dimensions={1}, use_global_device_ids=true | all-gather | bytes 557056 | tf_op jit(solution)/shard_map/all_gather | solution.py:57
  47.7 3.4 %collective-permute-start = (bf16[256,1024]{1,0:T(8,128)(2,1)S(1)}, bf16[256,1024]{1,0:T(8,128)(2,1)}, u32[]{:S(2)}, u32[]{:S(2)}) collective-permute-start(bf16[256,1024]{1,0:T(8,128)(2,1)S(1)} %bitcast.60), channel_id=1, source_target_pairs={{0,32},{32,64},{64,96},{96,0},{1,33},{33,65},{65,97},{97,1},{2,34}... | collective-permute-start | bytes 1572872 | tf_op jit(solution)/shard_map/ppermute | solution.py:28
  51.1 2.4 %collective-permute-start.2 = (bf16[256,1024]{1,0:T(8,128)(2,1)S(1)}, bf16[256,1024]{1,0:T(8,128)(2,1)}, u32[]{:S(2)}, u32[]{:S(2)}) collective-permute-start(bf16[256,1024]{1,0:T(8,128)(2,1)S(1)} %bitcast.61), channel_id=1, source_target_pairs={{0,96},{32,0},{64,32},{96,64},{1,97},{33,1},{65,33},{97,65},{2,98}... | collective-permute-start | bytes 1572872 | tf_op jit(solution)/shard_map/ppermute | solution.py:31
  53.6 0.0 copy-done
  53.6 1.3 gather_fusion.3
  54.9 0.7 gather_fusion.1
  55.6 0.1 select_reduce_fusion.1
  55.7 0.1 dynamic-slice_subtract_fusion
  55.8 0.1 tile.10
  55.9 0.1 select_reduce_fusion
  56.0 0.3 broadcast_and_fusion
  56.3 3.3 %collective-permute-done = bf16[256,1024]{1,0:T(8,128)(2,1)} collective-permute-done((bf16[256,1024]{1,0:T(8,128)(2,1)S(1)}, bf16[256,1024]{1,0:T(8,128)(2,1)}, u32[]{:S(2)}, u32[]{:S(2)}) %collective-permute-start) | collective-permute-done | bytes 524320 | tf_op jit(solution)/shard_map/ppermute | solution.py:28
  59.7 3.6 %collective-permute-start.1 = (bf16[256,1024]{1,0:T(8,128)(2,1)}, bf16[256,1024]{1,0:T(8,128)(2,1)}, u32[]{:S(2)}, u32[]{:S(2)}) collective-permute-start(bf16[256,1024]{1,0:T(8,128)(2,1)} %collective-permute-done), channel_id=1, source_target_pairs={{0,32},{32,64},{64,96},{96,0},{1,33},{33,65},{65,97},{97,1},{2,34}... | collective-permute-start | bytes 1572872 | tf_op jit(solution)/shard_map/ppermute | solution.py:28
  63.3 0.1 compare_select_fusion
  63.4 0.9 and.163
  64.3 0.0 copy-done.3
  64.3 1.5 %dynamic-slice_bitcast_fusion.2 = (f32[1024,256]{1,0:T(8,128)}, f32[1024,256]{1,0:T(8,128)}) fusion(f32[1,2048,256]{2,1,0:T(8,128)S(1)} %copy-done.3, s32[]{:T(128)S(6)} %select_n.191, s32[]{:T(128)S(6)} %select_n.171), kind=kLoop, calls=%fused_computation.16 | loop fusion | bytes 4194312 | tf_op jit(solution)/shard_map/dynamic_slice | solution.py:107
  65.8 0.0 collective-permute-done.2
  65.8 5.2 %collective-permute-done.1 = bf16[256,1024]{1,0:T(8,128)(2,1)} collective-permute-done((bf16[256,1024]{1,0:T(8,128)(2,1)}, bf16[256,1024]{1,0:T(8,128)(2,1)}, u32[]{:S(2)}, u32[]{:S(2)}) %collective-permute-start.1) | collective-permute-done | bytes 524320 | tf_op jit(solution)/shard_map/ppermute | solution.py:28
  71.0 2.9 %pad_maximum_fusion = bf16[4,256,1024]{2,1,0:T(8,128)(2,1)} fusion(bf16[1,256,1024]{2,1,0:T(8,128)(2,1)} %bitcast.4, bf16[1,256,1024]{2,1,0:T(8,128)(2,1)} %bitcast.3, bf16[1,256,1024]{2,1,0:T(8,128)(2,1)} %bitcast.2, bf16[1,256,1024]{2,1,0:T(8,128)(2,1)S(1)} %all-gather.1), kind=kLoop, calls=%fused_computation.9 | loop fusion | flops 3145728 | bytes 4194304 | tf_op jit(solution)/shard_map/stack | solution.py:37
  74.0 2.3 %gather_fusion = bf16[4,256,1024]{2,1,0:T(8,128)(2,1)S(1)} fusion(bf16[4,256,1024]{2,1,0:T(8,128)(2,1)} %pad_maximum_fusion, s32[1024]{0:T(1024)S(1)} %pad_clamp_fusion.5), kind=kCustom, calls=%fused_computation | custom fusion | bytes 4194320 | tf_op jit(solution)/shard_map/gather | solution.py:39
  76.3 12.4 %all-gather.5.cloned.1.call-done = bf16[1,2048,1024]{1,2,0:T(8,128)(2,1)} async-done(((bf16[1,2048,32]{1,2,0:T(8,128)(2,1)}), bf16[1,2048,1024]{1,2,0:T(8,128)(2,1)}) %all-gather.5.cloned.1.call-update) | async-done | bytes 4194320 | tf_op jit(solution)/shard_map/all_gather | solution.py:61
  88.7 1.6 %convolution_convert_fusion = bf16[64,1024]{1,0:T(8,128)(2,1)S(1)} fusion(bf16[1024,1024]{1,0:T(8,128)(2,1)S(1)} %bitcast.53, bf16[1,2048,1024]{1,2,0:T(8,128)(2,1)} %all-gather.5.cloned.1.call-done, s32[]{:T(128)S(6)} %select_n.180), kind=kOutput, calls=%fused_computation.14 | convolution fusion | flops 134283264 | bytes 2490372 | tf_op jit(solution)/shard_map/dot_general | solution.py:64
  90.2 1.4 %gather_fusion.2 = bf16[16,16,1024]{2,1,0:T(8,128)(2,1)} fusion(bf16[4,16,1024]{2,1,0:T(8,128)(2,1)S(1)} %bitcast.58, s32[1024]{0:T(1024)S(1)} %pad_clamp_fusion.3), kind=kCustom, calls=%fused_computation.2 | custom fusion | bytes 1048640 | tf_op jit(solution)/shard_map/gather | solution.py:92
  91.6 4.8 %all-to-all-start = ((bf16[4,64,1024]{2,1,0:T(8,128)(2,1)}), bf16[4,64,1024]{2,1,0:T(8,128)(2,1)S(1)}, u32[]{:S(2)}, u32[]{:S(2)}) async-start(bf16[4,64,1024]{2,1,0:T(8,128)(2,1)} %bitcast.14), calls=%async_computation | async-start | bytes 1048576 | tf_op jit(solution)/shard_map/all_to_all | solution.py:93
  96.4 7.0 %fusion.2 = bf16[1024,2048]{1,0:T(8,128)(2,1)S(1)} fusion(bf16[1024,1024]{1,0:T(8,128)(2,1)S(1)} %bitcast.54, bf16[1,2048,1024]{1,2,0:T(8,128)(2,1)} %all-gather.5.cloned.1.call-done), kind=kOutput, calls=%fused_computation.8 | convolution fusion | flops 4297064448 | bytes 10485760 | tf_op jit(solution)/shard_map/dot_general | solution.py:64
  103.4 1.8 %dynamic-slice_bitcast_fusion = (bf16[1024,1024]{0,1:T(8,128)(2,1)}, bf16[1024,1024]{0,1:T(8,128)(2,1)S(1)}) fusion(bf16[1024,2048]{1,0:T(8,128)(2,1)S(1)} %fusion.2, s32[]{:T(128)S(6)} %select_n.191, s32[]{:T(128)S(6)} %select_n.171), kind=kLoop, calls=%fused_computation.10 | loop fusion | bytes 8388616 | tf_op jit(solution)/shard_map/dynamic_slice | solution.py:108
  105.2 0.0 all-to-all-done
  105.2 0.0 copy-start.2
  105.2 2.5 %fusion.26 = f32[1024,256]{1,0:T(8,128)S(1)} fusion(bf16[1024,1024]{0,1:T(8,128)(2,1)} %get-tuple-element.12, bf16[256,1024]{1,0:T(8,128)(2,1)S(1)} %bitcast.55), kind=kOutput, calls=%fused_computation.87 | convolution fusion | flops 536870912 | bytes 3670016 | tf_op jit(solution)/shard_map/dot_general | solution.py:15
  107.7 0.0 copy-done.2
  107.7 0.7 convolution_subtract_fusion
  108.4 1.4 %gather_fusion.5 = bf16[64,16,256]{2,1,0:T(8,128)(2,1)} fusion(bf16[64,16,256]{2,1,0:T(8,128)(2,1)S(1)} %bitcast.59, s32[1024]{0:T(1024)S(1)} %pad_clamp_fusion), kind=kCustom, calls=%fused_computation.5 | custom fusion | bytes 1048832 | tf_op jit(solution)/shard_map/gather | solution.py:118
  109.8 0.0 copy-start.1
  109.8 3.6 %collective-permute-start.3 = (bf16[1024,256]{1,0:T(8,128)(2,1)}, bf16[1024,256]{1,0:T(8,128)(2,1)S(1)}, u32[]{:S(2)}, u32[]{:S(2)}) collective-permute-start(bf16[1024,256]{1,0:T(8,128)(2,1)} %bitcast.62), channel_id=1, source_target_pairs={{0,128},{128,0},{256,384},{384,256},{1,129},{129,1},{257,385},{385... | collective-permute-start | bytes 1572872 | tf_op jit(solution)/shard_map/ppermute | solution.py:11
  113.3 0.8 fusion.25
  114.1 0.0 copy-done.1
  114.1 0.7 convolution_subtract_fusion.1
  114.8 0.6 gather_fusion.4
  115.4 10.1 %collective-permute-done.3 = bf16[1024,256]{1,0:T(8,128)(2,1)S(1)} collective-permute-done((bf16[1024,256]{1,0:T(8,128)(2,1)}, bf16[1024,256]{1,0:T(8,128)(2,1)S(1)}, u32[]{:S(2)}, u32[]{:S(2)}) %collective-permute-start.3) | collective-permute-done | bytes 524320 | tf_op jit(solution)/shard_map/ppermute | solution.py:11
  125.5 1.1 bitcast_add_fusion
  (14 shorter events, 0.1 us)
Async XLA Ops:
  6.5 47.0 %copy-start = (s32[1,512]{1,0:T(1,128)S(1)}, s32[1,512]{1,0:T(1,128)}, u32[]{:S(2)}) copy-start(s32[1,512]{1,0:T(1,128)} %param.7) | copy-start | bytes 6148
  6.5 57.7 %copy-start.3 = (f32[1,2048,256]{2,1,0:T(8,128)S(1)}, f32[1,2048,256]{2,1,0:T(8,128)}, u32[]{:S(2)}) copy-start(f32[1,2048,256]{2,1,0:T(8,128)} %param.6) | copy-start | bytes 6291460
  6.5 82.1 %all-gather.5.cloned.1.call-start = ((), (), s32[]{:S(2)}) async-start(), calls=%async_computation.1 | async-start | bytes 4325376 | tf_op jit(solution)/shard_map/all_gather | solution.py:61
  47.7 12.0 %collective-permute-start = (bf16[256,1024]{1,0:T(8,128)(2,1)S(1)}, bf16[256,1024]{1,0:T(8,128)(2,1)}, u32[]{:S(2)}, u32[]{:S(2)}) collective-permute-start(bf16[256,1024]{1,0:T(8,128)(2,1)S(1)} %bitcast.60), channel_id=1, source_target_pairs={{0,32},{32,64},{64,96},{96,0},{1,33},{33,65},{65,97},{97,1},{2,34}... | collective-permute-start | bytes 1572872 | tf_op jit(solution)/shard_map/ppermute | solution.py:28
  51.1 14.7 %collective-permute-start.2 = (bf16[256,1024]{1,0:T(8,128)(2,1)S(1)}, bf16[256,1024]{1,0:T(8,128)(2,1)}, u32[]{:S(2)}, u32[]{:S(2)}) collective-permute-start(bf16[256,1024]{1,0:T(8,128)(2,1)S(1)} %bitcast.61), channel_id=1, source_target_pairs={{0,96},{32,0},{64,32},{96,64},{1,97},{33,1},{65,33},{97,65},{2,98}... | collective-permute-start | bytes 1572872 | tf_op jit(solution)/shard_map/ppermute | solution.py:31
  59.7 11.4 %collective-permute-start.1 = (bf16[256,1024]{1,0:T(8,128)(2,1)}, bf16[256,1024]{1,0:T(8,128)(2,1)}, u32[]{:S(2)}, u32[]{:S(2)}) collective-permute-start(bf16[256,1024]{1,0:T(8,128)(2,1)} %collective-permute-done), channel_id=1, source_target_pairs={{0,32},{32,64},{64,96},{96,0},{1,33},{33,65},{65,97},{97,1},{2,34}... | collective-permute-start | bytes 1572872 | tf_op jit(solution)/shard_map/ppermute | solution.py:28
  91.6 13.6 %all-to-all-start = ((bf16[4,64,1024]{2,1,0:T(8,128)(2,1)}), bf16[4,64,1024]{2,1,0:T(8,128)(2,1)S(1)}, u32[]{:S(2)}, u32[]{:S(2)}) async-start(bf16[4,64,1024]{2,1,0:T(8,128)(2,1)} %bitcast.14), calls=%async_computation | async-start | bytes 1048576 | tf_op jit(solution)/shard_map/all_to_all | solution.py:93
  105.2 2.5 %copy-start.2 = (f32[1024,256]{1,0:T(8,128)S(1)}, f32[1024,256]{1,0:T(8,128)}, u32[]{:S(2)}) copy-start(f32[1024,256]{1,0:T(8,128)} %get-tuple-element.11) | copy-start | bytes 3145732
  109.8 4.3 %copy-start.1 = (f32[1024,256]{1,0:T(8,128)S(1)}, f32[1024,256]{1,0:T(8,128)}, u32[]{:S(2)}) copy-start(f32[1024,256]{1,0:T(8,128)} %get-tuple-element.9) | copy-start | bytes 3145732
  109.8 15.7 %collective-permute-start.3 = (bf16[1024,256]{1,0:T(8,128)(2,1)}, bf16[1024,256]{1,0:T(8,128)(2,1)S(1)}, u32[]{:S(2)}, u32[]{:S(2)}) collective-permute-start(bf16[1024,256]{1,0:T(8,128)(2,1)} %bitcast.62), channel_id=1, source_target_pairs={{0,128},{128,0},{256,384},{384,256},{1,129},{129,1},{257,385},{385... | collective-permute-start | bytes 1572872 | tf_op jit(solution)/shard_map/ppermute | solution.py:11
Sparse Core Ops, SparseCore 0:
  9.5 79.1 all-gather.4
where the time goes:
time: 134 us; the launch traced here: 133 us
  blocking collectives  40.4 us (30%)
  waiting for transfers between devices  31.7 us (24%)
  starting transfers between devices  17.8 us (13%)
  between operations  13.7 us (10%)
  matrix products  13.1 us (10%)
  local copies, waits for them, and re-layouts  11.9 us (9%)
  other arithmetic  4.81 us (4%)
    all_gather x1, blocking collectives, local(): inverse = lax.all_gather(inverse, 'z', axis=0, tiled=True)  38.4 us
    all_gather x1, waiting for transfers between devices, local(): columns = lax.all_gather(panel[0], ('z', 'core'), axis=1, tiled=True)  12.4 us
    ppermute x1, waiting for transfers between devices, from_partner(): return lax.ppermute(value, axis, pairs)  10.1 us
    dot_general x2, matrix products, solve(): jnp.dot(rows, inverse, preferred_element_type=jnp.float32)  8.6 us
    ppermute x2, waiting for transfers between devices, ring_gather(): forward = lax.ppermute(forward, axis, ahead)  8.56 us
    ppermute x2, starting transfers between devices, ring_gather(): forward = lax.ppermute(forward, axis, ahead)  6.99 us
    all_to_all x1, starting transfers between devices, local(): lax.all_to_all(piece, 'row', 0, 0, tiled=True).reshape(cols_here, order)  4.78 us
    ppermute x1, starting transfers between devices, from_partner(): return lax.ppermute(value, axis, pairs)  3.55 us
  transfers between devices with their start and end apart: 6, of which 4 were waited for; matrix products, arithmetic and copies ran while one was open for 16% of the time, Pallas kernels for 0%

commit v1 on v0

--- a/solution.py
+++ b/solution.py
@@ -54,7 +54,10 @@
     row_index = lax.axis_index("row")
     col_index = lax.axis_index("z") * ncore + lax.axis_index("core")
     inverse = lax.all_gather(inverse_factor[0], "core", axis=0, tiled=True)
-    inverse = lax.all_gather(inverse, "z", axis=0, tiled=True)
+    current_value = lax.axis_size("z")
+    y = jnp.stack([inverse] * current_value, axis=0)
+    r2 = lax.all_to_all(y, "z", 0, 0)
+    inverse = jnp.concatenate(r2, axis=0)
     inverse = ring_gather(inverse, "row", row_index, nrow)
     order = inverse.shape[-1]
     inverse = inverse.reshape(order, order)

time: 134 us -> 145 us (1.082)
  the two profiles are of different devices: /device:TPU:2 before, /device:TPU:18 now
where the time goes in v1:
time: 145 us
  waiting for transfers between devices  66 us (46%)
  starting transfers between devices  32.1 us (22%)
  between operations  13.7 us (9%)
  matrix products  13.1 us (9%)
  local copies, waits for them, and re-layouts  12.7 us (9%)
  other arithmetic  4.84 us (3%)
  blocking collectives  2.04 us (1%)
    all_to_all x1, waiting for transfers between devices, local(): r2 = lax.all_to_all(y, 'z', 0, 0)  31.5 us
    all_to_all x1, starting transfers between devices, local(): r2 = lax.all_to_all(y, 'z', 0, 0)  15.2 us
    ppermute x2, waiting for transfers between devices, ring_gather(): forward = lax.ppermute(forward, axis, ahead)  14.8 us
    ppermute x1, waiting for transfers between devices, from_partner(): return lax.ppermute(value, axis, pairs)  10.8 us
    dot_general x2, matrix products, solve(): jnp.dot(rows, inverse, preferred_element_type=jnp.float32)  8.61 us
    all_gather x1, waiting for transfers between devices, local(): columns = lax.all_gather(panel[0], ('z', 'core'), axis=1, tiled=True)  8.22 us
    ppermute x2, starting transfers between devices, ring_gather(): forward = lax.ppermute(forward, axis, ahead)  6.76 us
    all_to_all x1, starting transfers between devices, local(): lax.all_to_all(piece, 'row', 0, 0, tiled=True).reshape(cols_here, order)  4.86 us
  transfers between devices with their start and end apart: 7, of which 5 were waited for; matrix products, arithmetic and copies ran while one was open for 15% of the time, Pallas kernels for 0%

profile of v1, /device:TPU:18, one launch (start us, length us, event | category | flops | bytes accessed | tf_op | source)
XLA Modules:
  0.0 144.6 jit_solution(10737000693869222942)
XLA Ops:
  6.5 0.0 copy-start
  6.5 0.0 copy-start.3
  6.5 0.0 all-gather.4.cloned.1.call-start
  6.5 0.7 all-gather.4.cloned.1.call-update
  7.3 2.0 %all-gather = bf16[1,16,1024]{2,1,0:T(8,128)(2,1)S(1)} all-gather(bf16[1,8,1024]{2,1,0:T(8,128)(2,1)} %param.4), channel_id=2, replica_groups=mesh['front'=4,'row'=4,'z'=16,'core'=2] {'core'}, dimensions={1}, use_global_device_ids=true | all-gather | bytes 49152 | tf_op jit(solution)/shard_map/all_gather | solution.py:56
  9.3 0.9 stack.10
  10.2 15.2 %all-to-all-start = ((bf16[16,16,1024]{2,1,0:T(8,128)(2,1)}), bf16[16,16,1024]{2,1,0:T(8,128)(2,1)S(1)}, u32[]{:S(2)}, u32[]{:S(2)}) async-start(bf16[16,16,1024]{2,1,0:T(8,128)(2,1)} %stack.10), calls=%async_computation | async-start | bytes 1048576 | tf_op jit(solution)/shard_map/all_to_all | solution.py:59
  25.4 0.0 copy-done
  25.4 1.3 gather_fusion.3
  26.7 0.7 gather_fusion.1
  27.4 0.1 select_reduce_fusion.1
  27.5 0.1 dynamic-slice_subtract_fusion
  27.6 0.1 tile.10
  27.7 0.1 select_reduce_fusion
  27.9 31.5 %all-to-all-done = bf16[16,16,1024]{2,1,0:T(8,128)(2,1)S(1)} async-done(((bf16[16,16,1024]{2,1,0:T(8,128)(2,1)}), bf16[16,16,1024]{2,1,0:T(8,128)(2,1)S(1)}, u32[]{:S(2)}, u32[]{:S(2)}) %all-to-all-start) | async-done | bytes 524320 | tf_op jit(solution)/shard_map/all_to_all | solution.py:59
  59.4 3.4 %collective-permute-start = (bf16[256,1024]{1,0:T(8,128)(2,1)S(1)}, bf16[256,1024]{1,0:T(8,128)(2,1)}, u32[]{:S(2)}, u32[]{:S(2)}) collective-permute-start(bf16[256,1024]{1,0:T(8,128)(2,1)S(1)} %bitcast.62), channel_id=1, source_target_pairs={{0,32},{32,64},{64,96},{96,0},{1,33},{33,65},{65,97},{97,1},{2,34}... | collective-permute-start | bytes 1572872 | tf_op jit(solution)/shard_map/ppermute | solution.py:28
  62.8 0.3 broadcast_and_fusion
  63.1 2.4 %collective-permute-start.2 = (bf16[256,1024]{1,0:T(8,128)(2,1)S(1)}, bf16[256,1024]{1,0:T(8,128)(2,1)}, u32[]{:S(2)}, u32[]{:S(2)}) collective-permute-start(bf16[256,1024]{1,0:T(8,128)(2,1)S(1)} %bitcast.63), channel_id=1, source_target_pairs={{0,96},{32,0},{64,32},{96,64},{1,97},{33,1},{65,33},{97,65},{2,98}... | collective-permute-start | bytes 1572872 | tf_op jit(solution)/shard_map/ppermute | solution.py:31
  65.6 9.3 %collective-permute-done = bf16[256,1024]{1,0:T(8,128)(2,1)} collective-permute-done((bf16[256,1024]{1,0:T(8,128)(2,1)S(1)}, bf16[256,1024]{1,0:T(8,128)(2,1)}, u32[]{:S(2)}, u32[]{:S(2)}) %collective-permute-start) | collective-permute-done | bytes 524320 | tf_op jit(solution)/shard_map/ppermute | solution.py:28
  74.9 3.4 %collective-permute-start.1 = (bf16[256,1024]{1,0:T(8,128)(2,1)}, bf16[256,1024]{1,0:T(8,128)(2,1)}, u32[]{:S(2)}, u32[]{:S(2)}) collective-permute-start(bf16[256,1024]{1,0:T(8,128)(2,1)} %collective-permute-done), channel_id=1, source_target_pairs={{0,32},{32,64},{64,96},{96,0},{1,33},{33,65},{65,97},{97,1},{2,34}... | collective-permute-start | bytes 1572872 | tf_op jit(solution)/shard_map/ppermute | solution.py:28
  78.3 0.1 compare_select_fusion
  78.4 0.9 and.163
  79.3 0.0 copy-done.3
  79.3 1.5 %dynamic-slice_bitcast_fusion.2 = (f32[1024,256]{1,0:T(8,128)}, f32[1024,256]{1,0:T(8,128)}) fusion(f32[1,2048,256]{2,1,0:T(8,128)S(1)} %copy-done.3, s32[]{:T(128)S(6)} %select_n.191, s32[]{:T(128)S(6)} %select_n.171), kind=kLoop, calls=%fused_computation.16 | loop fusion | bytes 4194312 | tf_op jit(solution)/shard_map/dynamic_slice | solution.py:110
  80.8 0.0 collective-permute-done.2
  80.8 5.5 %collective-permute-done.1 = bf16[256,1024]{1,0:T(8,128)(2,1)} collective-permute-done((bf16[256,1024]{1,0:T(8,128)(2,1)}, bf16[256,1024]{1,0:T(8,128)(2,1)}, u32[]{:S(2)}, u32[]{:S(2)}) %collective-permute-start.1) | collective-permute-done | bytes 524320 | tf_op jit(solution)/shard_map/ppermute | solution.py:28
  86.3 3.0 %pad_maximum_fusion = bf16[4,256,1024]{2,1,0:T(8,128)(2,1)} fusion(bf16[1,256,1024]{2,1,0:T(8,128)(2,1)} %bitcast.6, bf16[1,256,1024]{2,1,0:T(8,128)(2,1)} %bitcast.5, bf16[1,256,1024]{2,1,0:T(8,128)(2,1)} %bitcast.4, bf16[1,256,1024]{2,1,0:T(8,128)(2,1)S(1)} %bitcast.64), kind=kLoop, calls=%fused_computation.9 | loop fusion | flops 3145728 | bytes 4194304 | tf_op jit(solution)/shard_map/stack | solution.py:37
  89.3 2.3 %gather_fusion = bf16[4,256,1024]{2,1,0:T(8,128)(2,1)S(1)} fusion(bf16[4,256,1024]{2,1,0:T(8,128)(2,1)} %pad_maximum_fusion, s32[1024]{0:T(1024)S(1)} %pad_clamp_fusion.5), kind=kCustom, calls=%fused_computation | custom fusion | bytes 4194320 | tf_op jit(solution)/shard_map/gather | solution.py:39
  91.6 8.2 %all-gather.4.cloned.1.call-done = bf16[1,2048,1024]{1,2,0:T(8,128)(2,1)} async-done(((bf16[1,2048,32]{1,2,0:T(8,128)(2,1)}), bf16[1,2048,1024]{1,2,0:T(8,128)(2,1)}) %all-gather.4.cloned.1.call-update) | async-done | bytes 4194320 | tf_op jit(solution)/shard_map/all_gather | solution.py:64
  99.8 1.6 %convolution_convert_fusion = bf16[64,1024]{1,0:T(8,128)(2,1)S(1)} fusion(bf16[1024,1024]{1,0:T(8,128)(2,1)S(1)} %bitcast.55, bf16[1,2048,1024]{1,2,0:T(8,128)(2,1)} %all-gather.4.cloned.1.call-done, s32[]{:T(128)S(6)} %select_n.180), kind=kOutput, calls=%fused_computation.14 | convolution fusion | flops 134283264 | bytes 2490372 | tf_op jit(solution)/shard_map/dot_general | solution.py:67
  101.4 1.4 gather_fusion.2
  102.7 4.9 %all-to-all-start.1 = ((bf16[4,64,1024]{2,1,0:T(8,128)(2,1)}), bf16[4,64,1024]{2,1,0:T(8,128)(2,1)S(1)}, u32[]{:S(2)}, u32[]{:S(2)}) async-start(bf16[4,64,1024]{2,1,0:T(8,128)(2,1)} %bitcast.16), calls=%async_computation.1 | async-start | bytes 1048576 | tf_op jit(solution)/shard_map/all_to_all | solution.py:96
  107.6 7.0 %fusion.2 = bf16[1024,2048]{1,0:T(8,128)(2,1)S(1)} fusion(bf16[1024,1024]{1,0:T(8,128)(2,1)S(1)} %bitcast.56, bf16[1,2048,1024]{1,2,0:T(8,128)(2,1)} %all-gather.4.cloned.1.call-done), kind=kOutput, calls=%fused_computation.8 | convolution fusion | flops 4297064448 | bytes 10485760 | tf_op jit(solution)/shard_map/dot_general | solution.py:67
  114.6 1.8 %dynamic-slice_bitcast_fusion = (bf16[1024,1024]{0,1:T(8,128)(2,1)}, bf16[1024,1024]{0,1:T(8,128)(2,1)S(1)}) fusion(bf16[1024,2048]{1,0:T(8,128)(2,1)S(1)} %fusion.2, s32[]{:T(128)S(6)} %select_n.191, s32[]{:T(128)S(6)} %select_n.171), kind=kLoop, calls=%fused_computation.10 | loop fusion | bytes 8388616 | tf_op jit(solution)/shard_map/dynamic_slice | solution.py:111
  116.4 0.0 all-to-all-done.1
  116.4 0.0 copy-start.2
  116.4 2.5 %fusion.26 = f32[1024,256]{1,0:T(8,128)S(1)} fusion(bf16[1024,1024]{0,1:T(8,128)(2,1)} %get-tuple-element.12, bf16[256,1024]{1,0:T(8,128)(2,1)S(1)} %bitcast.57), kind=kOutput, calls=%fused_computation.87 | convolution fusion | flops 536870912 | bytes 3670016 | tf_op jit(solution)/shard_map/dot_general | solution.py:15
  118.9 0.0 copy-done.2
  118.9 0.7 convolution_subtract_fusion
  119.6 1.4 gather_fusion.5
  121.0 0.0 copy-start.1
  121.0 2.9 %collective-permute-start.3 = (bf16[1024,256]{1,0:T(8,128)(2,1)}, bf16[1024,256]{1,0:T(8,128)(2,1)S(1)}, u32[]{:S(2)}, u32[]{:S(2)}) collective-permute-start(bf16[1024,256]{1,0:T(8,128)(2,1)} %bitcast.65), channel_id=1, source_target_pairs={{0,128},{128,0},{256,384},{384,256},{1,129},{129,1},{257,385},{385... | collective-permute-start | bytes 1572872 | tf_op jit(solution)/shard_map/ppermute | solution.py:11
  123.8 0.8 fusion.25
  124.6 0.0 copy-done.1
  124.6 0.7 convolution_subtract_fusion.1
  125.3 0.6 gather_fusion.4
  125.9 10.8 %collective-permute-done.3 = bf16[1024,256]{1,0:T(8,128)(2,1)S(1)} collective-permute-done((bf16[1024,256]{1,0:T(8,128)(2,1)}, bf16[1024,256]{1,0:T(8,128)(2,1)S(1)}, u32[]{:S(2)}, u32[]{:S(2)}) %collective-permute-start.3) | collective-permute-done | bytes 524320 | tf_op jit(solution)/shard_map/ppermute | solution.py:11
  136.7 1.1 bitcast_add_fusion
  (14 shorter events, 0.1 us)
Async XLA Ops:
  6.5 18.9 %copy-start = (s32[1,512]{1,0:T(1,128)S(1)}, s32[1,512]{1,0:T(1,128)}, u32[]{:S(2)}) copy-start(s32[1,512]{1,0:T(1,128)} %param.7) | copy-start | bytes 6148
  6.5 72.7 %copy-start.3 = (f32[1,2048,256]{2,1,0:T(8,128)S(1)}, f32[1,2048,256]{2,1,0:T(8,128)}, u32[]{:S(2)}) copy-start(f32[1,2048,256]{2,1,0:T(8,128)} %param.6) | copy-start | bytes 6291460
  6.5 93.2 %all-gather.4.cloned.1.call-start = ((), (), s32[]{:S(2)}) async-start(), calls=%async_computation.2 | async-start | bytes 4325376 | tf_op jit(solution)/shard_map/all_gather | solution.py:64
  10.2 49.2 %all-to-all-start = ((bf16[16,16,1024]{2,1,0:T(8,128)(2,1)}), bf16[16,16,1024]{2,1,0:T(8,128)(2,1)S(1)}, u32[]{:S(2)}, u32[]{:S(2)}) async-start(bf16[16,16,1024]{2,1,0:T(8,128)(2,1)} %stack.10), calls=%async_computation | async-start | bytes 1048576 | tf_op jit(solution)/shard_map/all_to_all | solution.py:59
  59.4 15.5 %collective-permute-start = (bf16[256,1024]{1,0:T(8,128)(2,1)S(1)}, bf16[256,1024]{1,0:T(8,128)(2,1)}, u32[]{:S(2)}, u32[]{:S(2)}) collective-permute-start(bf16[256,1024]{1,0:T(8,128)(2,1)S(1)} %bitcast.62), channel_id=1, source_target_pairs={{0,32},{32,64},{64,96},{96,0},{1,33},{33,65},{65,97},{97,1},{2,34}... | collective-permute-start | bytes 1572872 | tf_op jit(solution)/shard_map/ppermute | solution.py:28
  63.1 17.7 %collective-permute-start.2 = (bf16[256,1024]{1,0:T(8,128)(2,1)S(1)}, bf16[256,1024]{1,0:T(8,128)(2,1)}, u32[]{:S(2)}, u32[]{:S(2)}) collective-permute-start(bf16[256,1024]{1,0:T(8,128)(2,1)S(1)} %bitcast.63), channel_id=1, source_target_pairs={{0,96},{32,0},{64,32},{96,64},{1,97},{33,1},{65,33},{97,65},{2,98}... | collective-permute-start | bytes 1572872 | tf_op jit(solution)/shard_map/ppermute | solution.py:31
  74.9 11.4 %collective-permute-start.1 = (bf16[256,1024]{1,0:T(8,128)(2,1)}, bf16[256,1024]{1,0:T(8,128)(2,1)}, u32[]{:S(2)}, u32[]{:S(2)}) collective-permute-start(bf16[256,1024]{1,0:T(8,128)(2,1)} %collective-permute-done), channel_id=1, source_target_pairs={{0,32},{32,64},{64,96},{96,0},{1,33},{33,65},{65,97},{97,1},{2,34}... | collective-permute-start | bytes 1572872 | tf_op jit(solution)/shard_map/ppermute | solution.py:28
  102.7 13.7 %all-to-all-start.1 = ((bf16[4,64,1024]{2,1,0:T(8,128)(2,1)}), bf16[4,64,1024]{2,1,0:T(8,128)(2,1)S(1)}, u32[]{:S(2)}, u32[]{:S(2)}) async-start(bf16[4,64,1024]{2,1,0:T(8,128)(2,1)} %bitcast.16), calls=%async_computation.1 | async-start | bytes 1048576 | tf_op jit(solution)/shard_map/all_to_all | solution.py:96
  116.4 2.5 %copy-start.2 = (f32[1024,256]{1,0:T(8,128)S(1)}, f32[1024,256]{1,0:T(8,128)}, u32[]{:S(2)}) copy-start(f32[1024,256]{1,0:T(8,128)} %get-tuple-element.11) | copy-start | bytes 3145732
  121.0 3.6 %copy-start.1 = (f32[1024,256]{1,0:T(8,128)S(1)}, f32[1024,256]{1,0:T(8,128)}, u32[]{:S(2)}) copy-start(f32[1024,256]{1,0:T(8,128)} %get-tuple-element.9) | copy-start | bytes 3145732
  121.0 15.7 %collective-permute-start.3 = (bf16[1024,256]{1,0:T(8,128)(2,1)}, bf16[1024,256]{1,0:T(8,128)(2,1)S(1)}, u32[]{:S(2)}, u32[]{:S(2)}) collective-permute-start(bf16[1024,256]{1,0:T(8,128)(2,1)} %bitcast.65), channel_id=1, source_target_pairs={{0,128},{128,0},{256,384},{384,256},{1,129},{129,1},{257,385},{385... | collective-permute-start | bytes 1572872 | tf_op jit(solution)/shard_map/ppermute | solution.py:11
Sparse Core Ops, SparseCore 0:
  9.5 90.2 all-gather.3
